TPU v7x, 32 devices: a whole 2x2x4 slice. The times are simulated.
32 devices in a mesh: tok: 8 (over z, x), grp: 4 (over y, core).
Axes of the slice: x: 2, y: 2, z: 4, core: 2. Of those that a mesh axis runs over, the one named last changes fastest.
Arguments:
- queries: bfloat16 [1536, 2048], P('tok', 'grp'), may hold values from -72 to 72
- new_keys: bfloat16 [1536, 2048], P('tok', 'grp'), may hold values from -8 to 8
- new_values: bfloat16 [1536, 2048], P('tok', 'grp'), may hold values from -6 to 6
- residual: bfloat16 [1536, 2048], P('tok', 'grp'), may hold values from -6 to 6
- w_out: bfloat16 [2048, 2048], P('grp'), may hold values from -0.125 to 0.125
- leaf_keys: bfloat16 [8, 512, 2048], P('tok', None, 'grp'), may hold values from -6 to 6
- leaf_values: bfloat16 [8, 512, 2048], P('tok', None, 'grp'), may hold values from -6 to 6
- upper_keys: bfloat16 [6, 1024, 2048], P(None, 'tok', 'grp'), may hold values from -8 to 8
- upper_values: bfloat16 [6, 1024, 2048], P(None, 'tok', 'grp'), may hold values from -6 to 6
- req_len: int32 [8], replicated, may hold values from 48 to 192, as said below
- leaf_mid: int32 [8], replicated, may hold values from 0 to 3
- mid_root: int32 [4], replicated, may hold values from 0 to 1, as said below
- upper_len: int32 [6], replicated, may hold values from 256 to 1024, as said below
- leaf_len: int32 [8], replicated, may hold values from 128 to 512, as said below
Outputs:
- hidden_out: bfloat16 [1536, 2048], P('tok', 'grp')
Inputs may be any that keep to these rules, and one draw needn't show every extreme that they name: `req_len`: some request has exactly 192 new tokens. `mid_root`: each root is the parent of 2 mids. `upper_len`: the first 2 entries are roots and equal 1024. `leaf_len`: some leaf has exactly 512 positions.
All inputs are finite; a program needn't handle non-finite values.
Results may differ from a plain program's by a relative error of at most 0.008.
Values may be sent and summed in bfloat16 or wider, within the bound.
No kernel may reach another device: no remote copies, remote signals or barrier semaphores. Data moves between devices by JAX's collectives and lax.ppermute only.
A program may use at most 64 MiB of HBM per device.

v0:
```python
import math
import jax
import jax.numpy as jnp
from jax import lax
from jax.sharding import PartitionSpec as P

HEAD_DIM = 128
NEG_FILL = -1e30


def partial_attention(query_rows, key_rows, values, allowed, head_count):
    head_width = query_rows.shape[1] // head_count
    query_heads = query_rows.reshape(query_rows.shape[0], head_count, head_width)
    key_heads = key_rows.reshape(key_rows.shape[0], head_count, head_width)
    value_heads = values.reshape(values.shape[0], head_count, head_width)
    scores = jnp.einsum(
        "qhd,khd->hqk", query_heads, key_heads, preferred_element_type=jnp.float32
    ) * head_width ** (-0.5)
    scores = jnp.where(allowed[None], scores, NEG_FILL)
    row_max = jnp.max(scores, axis=2)
    exp_scores = jnp.where(allowed[None], jnp.exp(scores - row_max[:, :, None]), 0.0)
    row_total = jnp.sum(exp_scores, axis=2)
    weighted = jnp.einsum(
        "hqk,khd->hqd",
        exp_scores.astype(jnp.bfloat16),
        value_heads,
        preferred_element_type=jnp.float32,
    )
    return (row_max, row_total, weighted)


def combine(earlier, latter):
    new_max = jnp.maximum(earlier[0], latter[0])
    earlier_scale = jnp.exp(earlier[0] - new_max)
    latter_scale = jnp.exp(latter[0] - new_max)
    return (
        new_max,
        earlier[1] * earlier_scale + latter[1] * latter_scale,
        earlier[2] * earlier_scale[:, :, None] + latter[2] * latter_scale[:, :, None],
    )


def node_attention(carry, query_rows, node_keys, node_values, node_len, head_count):
    node_rows = node_keys.shape[0]
    block = math.gcd(node_rows, 512)
    row_count = query_rows.shape[0]
    for start in range(0, node_rows, block):
        positions = start + jnp.arange(block, dtype=jnp.int32)
        allowed = jnp.broadcast_to((positions < node_len)[None, :], (row_count, block))
        piece_part = partial_attention(
            query_rows,
            node_keys[start : start + block],
            node_values[start : start + block],
            allowed,
            head_count,
        )
        carry = combine(carry, piece_part)
    return carry


def shards(
    queries,
    new_keys,
    new_values,
    residual,
    w_out,
    leaf_keys,
    leaf_values,
    upper_keys,
    upper_values,
    req_len,
    leaf_mid,
    mid_root,
    upper_len,
    leaf_len,
):
    dev_count = lax.axis_size("tok")
    my_index = lax.axis_index("tok")
    row_count = queries.shape[0]
    col_count = queries.shape[1]
    head_count = col_count // HEAD_DIM
    mid_count = mid_root.shape[0]
    node_count = upper_len.shape[0]
    root_count = node_count - mid_count
    owned = (jnp.arange(dev_count, dtype=jnp.int32) == my_index).astype(jnp.int32)
    my_length = jnp.sum(owned * req_len)
    my_mid = jnp.sum(owned * leaf_mid)
    my_leaf_len = jnp.sum(owned * leaf_len)
    my_root = jnp.sum((jnp.arange(mid_count) == my_mid).astype(jnp.int32) * mid_root)
    node_ids = jnp.arange(node_count)
    root_len = jnp.sum((node_ids == my_root).astype(jnp.int32) * upper_len)
    mid_len = jnp.sum((node_ids == root_count + my_mid).astype(jnp.int32) * upper_len)
    position = jnp.arange(row_count, dtype=jnp.int32)
    is_live = position < my_length
    leaf_count = leaf_keys.shape[1]
    local_keys = jnp.concatenate([leaf_keys[0], new_keys], axis=0)
    local_values = jnp.concatenate([leaf_values[0], new_values], axis=0)
    leaf_allowed = jnp.broadcast_to(
        (jnp.arange(leaf_count) < my_leaf_len)[None, :], (row_count, leaf_count)
    )
    new_allowed = (position[None, :] <= position[:, None]) & is_live[None, :]
    local_part = partial_attention(
        queries,
        local_keys,
        local_values,
        jnp.concatenate([leaf_allowed, new_allowed], axis=1),
        head_count,
    )
    gathered_keys, gathered_values = (
        lax.all_gather(upper_keys, "tok", axis=1, tiled=True),
        lax.all_gather(upper_values, "tok", axis=1, tiled=True),
    )
    merged = node_attention(
        local_part, queries, gathered_keys[my_root], gathered_values[my_root], root_len, head_count
    )
    merged = node_attention(
        merged,
        queries,
        gathered_keys[root_count + my_mid],
        gathered_values[root_count + my_mid],
        mid_len,
        head_count,
    )
    attended = (merged[2] / merged[1][:, :, None]).transpose(1, 0, 2).reshape(row_count, col_count)
    attention = jnp.where(is_live[:, None], attended, 0.0).astype(jnp.bfloat16)
    projected = jnp.dot(attention, w_out, preferred_element_type=jnp.float32)
    mixed = lax.psum_scatter(
        projected.astype(jnp.bfloat16), "grp", scatter_dimension=1, tiled=True
    ).astype(jnp.float32)
    return (residual.astype(jnp.float32) + mixed).astype(jnp.bfloat16)


def solution(mesh):
    in_specs = (
        P("tok", "grp"),
        P("tok", "grp"),
        P("tok", "grp"),
        P("tok", "grp"),
        P("grp", None),
        P("tok", None, "grp"),
        P("tok", None, "grp"),
        P(None, "tok", "grp"),
        P(None, "tok", "grp"),
        P(),
        P(),
        P(),
        P(),
        P(),
    )
    out_specs = P("tok", "grp")
    return jax.shard_map(shards, mesh=mesh, in_specs=in_specs, out_specs=out_specs, check_vma=False)
```

profile of v0, /device:TPU:0, one launch (start us, length us, event | category | flops | bytes accessed | tf_op | source)
XLA Modules:
  0.0 251.3 jit_solution(10677370438847150841)
XLA Ops:
  6.5 0.0 copy-start
  6.5 0.0 all-gather.3.cloned.1.call-start
  6.5 2.5 copy.27
  9.0 0.0 all-gather.3.cloned.1.call-update
  9.0 0.0 all-gather.5.cloned.1.call-start
  9.1 0.0 copy-done.12
  9.1 1.2 copy.30
  10.3 0.0 all-gather.5.cloned.1.call-update
  10.3 0.0 reduce-scatter.2.cloned.1.call-start
  10.4 0.0 copy-done.16
  10.4 0.6 select_reduce_fusion
  12.3 1.3 fusion.91
  14.9 0.2 copy.20
  15.1 0.0 copy-start.18
  15.1 0.0 copy-start.20
  15.1 0.0 copy-start.14
  15.1 1.0 copy.21
  16.2 1.3 copy.24
  17.4 0.3 copy.25
  18.3 0.6 iota_compare_fusion.3
  18.9 1.2 fusion.92
  20.2 0.6 iota_compare_fusion.1
  20.8 0.6 fusion.89
  21.4 0.7 fusion.90
  22.0 0.7 iota_compare_fusion.2
  22.7 0.6 select_reduce_fusion.2
  23.3 0.6 iota_compare_fusion.4
  24.0 0.1 pad_add_fusion
  24.1 1.0 copy_bitcast_fusion
  25.1 0.0 copy-done.9
  25.1 1.7 fusion
  26.9 1.4 copy-done.10
  28.3 0.9 fusion.1
  29.1 82.9 %all-gather.3.cloned.1.call-done = bf16[6,1024,512]{1,2,0:T(8,128)(2,1)} async-done(((bf16[6,128,512]{1,2,0:T(8,128)(2,1)}), bf16[6,1024,512]{1,2,0:T(8,128)(2,1)}) %all-gather.3.cloned.1.call-update) | async-done | bytes 6291472 | tf_op jit(solution)/shard_map/all_gather | solution.py:110
  112.1 1.7 constant_dynamic-slice_fusion.3
  113.7 0.5 bitcast_reduce_fusion
  114.2 0.5 fusion.17
  114.7 0.5 bitcast_reduce_fusion.1
  115.2 0.1 copy-done.3
  115.3 0.5 fusion.15
  115.9 0.5 bitcast_reduce_fusion.2
  116.3 0.2 copy-done.5
  116.5 0.5 fusion.13
  117.0 0.5 bitcast_reduce_fusion.3
  117.5 0.2 copy-done.1
  117.7 1.1 copy-done.7
  118.9 0.5 fusion.11
  119.4 92.8 %all-gather.5.cloned.1.call-done = bf16[6,1024,512]{1,2,0:T(8,128)(2,1)} async-done(((bf16[6,128,512]{1,2,0:T(8,128)(2,1)}), bf16[6,1024,512]{1,2,0:T(8,128)(2,1)}) %all-gather.5.cloned.1.call-update) | async-done | bytes 6291472 | tf_op jit(solution)/shard_map/all_gather | solution.py:111
  212.3 1.8 constant_dynamic-slice_fusion.4
  214.1 0.3 copy-done.6
  214.3 0.5 fusion.22
  214.8 0.7 copy-done.8
  215.5 0.5 fusion.24
  216.0 0.6 copy-done.11
  216.6 1.0 fusion.31
  217.5 0.4 copy-done.2
  218.0 0.6 fusion.32
  218.5 0.8 copy-done.4
  219.4 0.5 fusion.30
  219.9 0.0 copy-start.15
  219.9 1.5 convolution_convert_fusion
  221.4 0.0 reduce-scatter.2.cloned.1.call-update
  221.4 21.6 %reduce-scatter.2.cloned.1.call-done = bf16[192,512]{1,0:T(8,128)(2,1)} async-done(((bf16[192,2048]{1,0:T(8,128)(2,1)}), bf16[192,512]{1,0:T(8,128)(2,1)}) %reduce-scatter.2.cloned.1.call-update) | async-done | bytes 196624 | tf_op jit(solution)/shard_map/reduce_scatter | solution.py:127
  243.1 1.7 add_convert_fusion
  (28 shorter events, 0.1 us)
Async XLA Ops:
  6.5 213.3 %copy-start = (bf16[512,2048]{1,0:T(8,128)(2,1)S(1)}, bf16[512,2048]{1,0:T(8,128)(2,1)}, u32[]{:S(2)}) copy-start(bf16[512,2048]{1,0:T(8,128)(2,1)} %param.18) | copy-start | bytes 6291460
  6.5 2.6 %copy-start.12 = (bf16[6,128,512]{2,1,0:T(8,128)(2,1)S(1)}, bf16[6,128,512]{2,1,0:T(8,128)(2,1)}, u32[]{:S(2)}) copy-start(bf16[6,128,512]{2,1,0:T(8,128)(2,1)} %param.22) | copy-start | bytes 2359300
  6.5 105.5 %all-gather.3.cloned.1.call-start = ((), (), s32[]{:S(2)}) async-start(), calls=%async_computation.1 | async-start | bytes 7077888 | tf_op jit(solution)/shard_map/all_gather | solution.py:110
  9.0 1.3 copy-start.16
  9.0 1.4 copy-start.17
  9.0 3.3 %copy-start.19 = (s32[4]{0:T(128)S(1)}, s32[4]{0:T(128)}, u32[]{:S(2)}) copy-start(s32[4]{0:T(128)} %param.25) | copy-start | bytes 52
  9.0 5.8 %copy-start.13 = (bf16[1,512,512]{2,1,0:T(8,128)(2,1)S(1)}, bf16[1,512,512]{2,1,0:T(8,128)(2,1)}, u32[]{:S(2)}) copy-start(bf16[1,512,512]{2,1,0:T(8,128)(2,1)} %param.19) | copy-start | bytes 1572868
  9.0 203.2 %all-gather.5.cloned.1.call-start = ((), (), s32[]{:S(2)}) async-start(), calls=%async_computation.2 | async-start | bytes 7077888 | tf_op jit(solution)/shard_map/all_gather | solution.py:111
  10.3 232.8 %reduce-scatter.2.cloned.1.call-start = ((), (), s32[]{:S(2)}) async-start(), calls=%async_computation.3 | async-start | bytes 983040 | tf_op jit(solution)/shard_map/reduce_scatter | solution.py:127
  15.1 3.9 %copy-start.18 = (s32[6]{0:T(128)S(1)}, s32[6]{0:T(128)}, u32[]{:S(2)}) copy-start(s32[6]{0:T(128)} %param.26) | copy-start | bytes 76
  15.1 7.6 %copy-start.20 = (s32[8]{0:T(128)S(1)}, s32[8]{0:T(128)}, u32[]{:S(2)}) copy-start(s32[8]{0:T(128)} %param.23) | copy-start | bytes 100
  15.1 9.0 %copy-start.14 = (bf16[192,512]{1,0:T(8,128)(2,1)S(1)}, bf16[192,512]{1,0:T(8,128)(2,1)}, u32[]{:S(2)}) copy-start(bf16[192,512]{1,0:T(8,128)(2,1)} %param.15) | copy-start | bytes 589828
  16.2 8.9 %copy-start.9 = (bf16[192,512]{1,0:T(8,128)(2,1)S(1)}, bf16[192,512]{1,0:T(8,128)(2,1)}, u32[]{:S(2)}) copy-start(bf16[192,512]{1,0:T(8,128)(2,1)} %param.14) | copy-start | bytes 589828
  26.8 1.4 copy-start.10
  114.2 1.2 copy-start.3
  115.3 1.2 copy-start.5
  116.5 1.2 copy-start.1
  117.7 1.1 copy-start.7
  212.3 2.0 copy-start.6
  214.0 1.5 copy-start.8
  214.8 1.8 copy-start.11
  216.6 1.4 copy-start.2
  218.0 1.4 copy-start.4
  219.9 23.2 %copy-start.15 = (bf16[192,512]{1,0:T(8,128)(2,1)S(1)}, bf16[192,512]{1,0:T(8,128)(2,1)}, u32[]{:S(2)}) copy-start(bf16[192,512]{1,0:T(8,128)(2,1)} %param.17) | copy-start | bytes 589828
Sparse Core Ops, SparseCore 0:
  9.4 102.6 all-gather.2
  114.1 98.1 all-gather.4
  221.6 21.4 reduce-scatter.1
where the time goes:
time: 252 us; the launch traced here: 251 us
  waiting for transfers between devices  197 us (78%)
  local copies, waits for them, and re-layouts  16.9 us (7%)
  between operations  16.5 us (7%)
  other arithmetic  12.3 us (5%)
  matrix products  8.03 us (3%)
    all_gather x1, waiting for transfers between devices, shards(): lax.all_gather(upper_values, 'tok', axis=1, tiled=True)  92.8 us
    all_gather x1, waiting for transfers between devices, shards(): lax.all_gather(upper_keys, 'tok', axis=1, tiled=True)  82.9 us
    reduce_scatter x1, waiting for transfers between devices, shards(): lax.psum_scatter(projected.astype(jnp.bfloat16), 'grp', scatter_dimension...  21.6 us
    unnamed x46, local copies, waits for them, and re-layouts  11.2 us
  transfers between devices with their start and end apart: 3, of which 3 were waited for; matrix products, arithmetic and copies ran while one was open for 8% of the time, Pallas kernels for 0%

commit v1 on v0

--- a/solution.py
+++ b/solution.py
@@ -3,6 +3,7 @@
 import jax.numpy as jnp
 from jax import lax
 from jax.sharding import PartitionSpec as P
+from jax.lax import axis_index, axis_size, ppermute
 
 HEAD_DIM = 128
 NEG_FILL = -1e30
@@ -106,8 +107,20 @@
         jnp.concatenate([leaf_allowed, new_allowed], axis=1),
         head_count,
     )
+
+    def do_slots(array_here, named_axis):
+        field_out, z2 = (axis_size(named_axis), axis_index(named_axis))
+        seen_now, back = (array_here, 1)
+        while back < field_out:
+            plain = ppermute(seen_now, named_axis, [(p, p ^ back) for p in range(field_out)])
+            odd = jnp.concatenate([seen_now, plain], axis=1)
+            y_new = jnp.concatenate([plain, seen_now], axis=1)
+            seen_now = jnp.where(z2 & back == 0, odd, y_new)
+            back = 2 * back
+        return seen_now
+
     gathered_keys, gathered_values = (
-        lax.all_gather(upper_keys, "tok", axis=1, tiled=True),
+        do_slots(upper_keys, "tok"),
         lax.all_gather(upper_values, "tok", axis=1, tiled=True),
     )
     merged = node_attention(

time: 252 us -> 333 us (1.32)
  waiting for transfers between devices: 197 us -> 260 us
  other arithmetic: 12.3 us -> 27.4 us
  starting transfers between devices: 0.09 us -> 5.35 us
    ppermute x0 -> x3, waiting for transfers between devices: none -> 238 us  [do_slots(): ppermute(seen_now, named_axis, [(p, p ^ back) for p in range(field_out)])]
    all_gather x1, waiting for transfers between devices: 92.8 us -> 0.02 us  [shards(): lax.all_gather(upper_values, 'tok', axis=1, tiled=True)]
    all_gather x1 -> x0, waiting for transfers between devices: 82.9 us -> none  [shards(): lax.all_gather(upper_keys, 'tok', axis=1, tiled=True)]
    select_n x0 -> x3, other arithmetic: none -> 15.2 us  [do_slots(): seen_now = jnp.where(z2 & back == 0, odd, y_new)]
    ppermute x0 -> x3, starting transfers between devices: none -> 5.3 us  [do_slots(): ppermute(seen_now, named_axis, [(p, p ^ back) for p in range(field_out)])]
    unnamed x46 -> x44, local copies, waits for them, and re-layouts: 11.2 us -> 10.6 us
  transfers between devices with their start and end apart: 3 -> 5, of which waited for: 3 -> 4; matrix products, arithmetic and copies ran while one was open for 8% -> 11% of each run, Pallas kernels for 0% -> 0%
where the time goes in v1:
time: 333 us; the launch traced here: 332 us
  waiting for transfers between devices  260 us (78%)
  other arithmetic  27.4 us (8%)
  between operations  16.9 us (5%)
  local copies, waits for them, and re-layouts  14.9 us (4%)
  matrix products  8.02 us (2%)
  starting transfers between devices  5.35 us (2%)
    ppermute x3, waiting for transfers between devices, do_slots(): ppermute(seen_now, named_axis, [(p, p ^ back) for p in range(field_out)])  238 us
    reduce_scatter x1, waiting for transfers between devices, shards(): lax.psum_scatter(projected.astype(jnp.bfloat16), 'grp', scatter_dimension...  21.1 us
    select_n x3, other arithmetic, do_slots(): seen_now = jnp.where(z2 & back == 0, odd, y_new)  15.2 us
    unnamed x44, local copies, waits for them, and re-layouts  10.6 us
  transfers between devices with their start and end apart: 5, of which 4 were waited for; matrix products, arithmetic and copies ran while one was open for 11% of the time, Pallas kernels for 0%

profile of v1, /device:TPU:0, one launch (start us, length us, event | category | flops | bytes accessed | tf_op | source)
XLA Modules:
  0.0 332.2 jit_solution(11666580835793956953)
XLA Ops:
  6.5 2.4 copy.32
  9.0 0.0 all-gather.2.cloned.1.call-update
  9.0 0.0 reduce-scatter.2.cloned.1.call-start
  9.1 1.5 copy.28
  10.6 3.0 collective-permute-start
  13.6 26.1 %collective-permute-done = bf16[6,128,512]{1,2,0:T(8,128)(2,1)} collective-permute-done((bf16[6,128,512]{1,2,0:T(8,128)(2,1)S(1)}, bf16[6,128,512]{1,2,0:T(8,128)(2,1)}, u32[]{:S(2)}, u32[]{:S(2)}) %collective-permute-start) | collective-permute-done | bytes 786464 | tf_op jit(solution)/shard_map/ppermute | solution.py:115
  39.7 3.1 maximum_select_fusion.2
  42.7 1.8 collective-permute-start.1
  44.6 69.3 %collective-permute-done.1 = bf16[6,256,512]{1,2,0:T(8,128)(2,1)} collective-permute-done((bf16[6,256,512]{1,2,0:T(8,128)(2,1)}, bf16[6,256,512]{1,2,0:T(8,128)(2,1)}, u32[]{:S(2)}, u32[]{:S(2)}) %collective-permute-start.1) | collective-permute-done | bytes 1572896 | tf_op jit(solution)/shard_map/ppermute | solution.py:115
  113.9 4.9 %maximum_select_fusion.1 = bf16[6,512,512]{1,2,0:T(8,128)(2,1)} fusion(bf16[6,256,512]{1,2,0:T(8,128)(2,1)} %collective-permute-done.1, bf16[6,256,512]{1,2,0:T(8,128)(2,1)} %maximum_select_fusion.2, pred[]{:T(512)S(6)} %eq.40), kind=kLoop, calls=%fused_computation.1 | loop fusion | flops 14155776 | bytes 6291457 | tf_op jit(solution)/shard_map/jit(_where)/select_n | solution.py:118
  118.8 0.5 collective-permute-start.2
  119.2 0.6 select_reduce_fusion
  121.2 1.3 fusion.91
  123.7 0.2 copy.20
  124.0 0.0 copy-start.17
  124.0 0.0 copy-start.19
  124.0 0.0 copy-start.13
  124.0 1.0 copy.21
  125.0 1.3 copy.24
  126.3 0.3 copy.25
  127.2 0.6 iota_compare_fusion.3
  127.8 1.2 fusion.92
  129.1 0.6 iota_compare_fusion.1
  129.7 0.6 fusion.89
  130.2 0.7 fusion.90
  130.9 0.7 iota_compare_fusion.2
  131.6 0.6 select_reduce_fusion.2
  132.2 0.6 iota_compare_fusion.4
  132.9 0.1 pad_add_fusion
  133.0 1.0 copy_bitcast_fusion
  134.0 1.7 fusion
  135.7 0.9 fusion.1
  136.6 0.6 copy-done.10
  137.2 143.0 %collective-permute-done.2 = bf16[6,512,512]{1,2,0:T(8,128)(2,1)} collective-permute-done((bf16[6,512,512]{1,2,0:T(8,128)(2,1)}, bf16[6,512,512]{1,2,0:T(8,128)(2,1)}, u32[]{:S(2)}, u32[]{:S(2)}) %collective-permute-start.2) | collective-permute-done | bytes 3145760 | tf_op jit(solution)/shard_map/ppermute | solution.py:115
  280.2 7.2 %maximum_select_fusion = bf16[6,1024,512]{1,2,0:T(8,128)(2,1)S(1)} fusion(bf16[6,512,512]{1,2,0:T(8,128)(2,1)} %collective-permute-done.2, bf16[6,512,512]{1,2,0:T(8,128)(2,1)} %maximum_select_fusion.1, pred[]{:T(512)S(6)} %eq.39), kind=kLoop, calls=%fused_computation | loop fusion | flops 28311552 | bytes 12582913 | tf_op jit(solution)/shard_map/jit(_where)/select_n | solution.py:118
  287.4 0.2 constant_dynamic-slice_fusion.3
  287.6 0.5 bitcast_reduce_fusion
  288.1 0.5 fusion.17
  288.6 0.5 bitcast_reduce_fusion.1
  289.1 0.1 copy-done.3
  289.2 0.5 fusion.15
  289.8 0.5 bitcast_reduce_fusion.2
  290.2 0.2 copy-done.5
  290.4 0.5 fusion.13
  291.0 0.5 bitcast_reduce_fusion.3
  291.4 0.2 copy-done.1
  291.7 1.1 copy-done.7
  292.8 0.5 fusion.11
  293.4 0.0 all-gather.2.cloned.1.call-done
  293.4 1.8 constant_dynamic-slice_fusion.4
  295.2 0.2 copy-done.6
  295.4 0.5 fusion.22
  295.9 0.7 copy-done.8
  296.6 0.5 fusion.24
  297.1 0.6 copy-done.11
  297.7 1.0 fusion.31
  298.6 0.4 copy-done.2
  299.1 0.6 fusion.32
  299.6 0.8 copy-done.4
  300.5 0.5 fusion.30
  301.0 1.5 convolution_convert_fusion
  302.5 0.0 reduce-scatter.2.cloned.1.call-update
  302.6 21.1 %reduce-scatter.2.cloned.1.call-done = bf16[192,512]{1,0:T(8,128)(2,1)} async-done(((bf16[192,2048]{1,0:T(8,128)(2,1)}), bf16[192,512]{1,0:T(8,128)(2,1)}) %reduce-scatter.2.cloned.1.call-update) | async-done | bytes 196624 | tf_op jit(solution)/shard_map/reduce_scatter | solution.py:140
  323.7 1.7 add_convert_fusion
  (32 shorter events, 0.1 us)
Async XLA Ops:
  6.5 294.5 %copy-start = (bf16[512,2048]{1,0:T(8,128)(2,1)S(1)}, bf16[512,2048]{1,0:T(8,128)(2,1)}, u32[]{:S(2)}) copy-start(bf16[512,2048]{1,0:T(8,128)(2,1)} %param.18) | copy-start | bytes 6291460
  6.5 286.8 %all-gather.2.cloned.1.call-start = ((), (), s32[]{:S(2)}) async-start(), calls=%async_computation.1 | async-start | bytes 7077888 | tf_op jit(solution)/shard_map/all_gather | solution.py:124
  9.0 314.7 %reduce-scatter.2.cloned.1.call-start = ((), (), s32[]{:S(2)}) async-start(), calls=%async_computation.2 | async-start | bytes 983040 | tf_op jit(solution)/shard_map/reduce_scatter | solution.py:140
  10.6 29.1 %collective-permute-start = (bf16[6,128,512]{1,2,0:T(8,128)(2,1)S(1)}, bf16[6,128,512]{1,2,0:T(8,128)(2,1)}, u32[]{:S(2)}, u32[]{:S(2)}) collective-permute-start(bf16[6,128,512]{1,2,0:T(8,128)(2,1)S(1)} %copy.28), channel_id=1, source_target_pairs={{0,4},{4,0},{8,12},{12,8},{16,20},{20,16},{24,28},{28,24},{1,5},{5... | collective-permute-start | bytes 2359304 | tf_op jit(solution)/shard_map/ppermute | solution.py:115
  42.7 71.2 %collective-permute-start.1 = (bf16[6,256,512]{1,2,0:T(8,128)(2,1)}, bf16[6,256,512]{1,2,0:T(8,128)(2,1)}, u32[]{:S(2)}, u32[]{:S(2)}) collective-permute-start(bf16[6,256,512]{1,2,0:T(8,128)(2,1)} %maximum_select_fusion.2), channel_id=1, source_target_pairs={{0,8},{4,12},{8,0},{12,4},{16,24},{20,28},{24,16},{28,20},{1,9},{5... | collective-permute-start | bytes 4718600 | tf_op jit(solution)/shard_map/ppermute | solution.py:115
  44.6 74.7 %copy-start.15 = (s32[8]{0:T(128)S(1)}, s32[8]{0:T(128)}, u32[]{:S(2)}) copy-start(s32[8]{0:T(128)} %param.24) | copy-start | bytes 100
  44.6 74.7 %copy-start.16 = (s32[8]{0:T(128)S(1)}, s32[8]{0:T(128)}, u32[]{:S(2)}) copy-start(s32[8]{0:T(128)} %param.27) | copy-start | bytes 100
  44.6 76.6 %copy-start.18 = (s32[4]{0:T(128)S(1)}, s32[4]{0:T(128)}, u32[]{:S(2)}) copy-start(s32[4]{0:T(128)} %param.25) | copy-start | bytes 52
  44.6 79.2 %copy-start.12 = (bf16[1,512,512]{2,1,0:T(8,128)(2,1)S(1)}, bf16[1,512,512]{2,1,0:T(8,128)(2,1)}, u32[]{:S(2)}) copy-start(bf16[1,512,512]{2,1,0:T(8,128)(2,1)} %param.19) | copy-start | bytes 1572868
  118.8 161.4 %collective-permute-start.2 = (bf16[6,512,512]{1,2,0:T(8,128)(2,1)}, bf16[6,512,512]{1,2,0:T(8,128)(2,1)}, u32[]{:S(2)}, u32[]{:S(2)}) collective-permute-start(bf16[6,512,512]{1,2,0:T(8,128)(2,1)} %maximum_select_fusion.1), channel_id=1, source_target_pairs={{0,16},{4,20},{8,24},{12,28},{16,0},{20,4},{24,8},{28,12},{1,17},{... | collective-permute-start | bytes 9437192 | tf_op jit(solution)/shard_map/ppermute | solution.py:115
  124.0 3.9 %copy-start.17 = (s32[6]{0:T(128)S(1)}, s32[6]{0:T(128)}, u32[]{:S(2)}) copy-start(s32[6]{0:T(128)} %param.26) | copy-start | bytes 76
  124.0 7.6 %copy-start.19 = (s32[8]{0:T(128)S(1)}, s32[8]{0:T(128)}, u32[]{:S(2)}) copy-start(s32[8]{0:T(128)} %param.23) | copy-start | bytes 100
  124.0 9.0 %copy-start.13 = (bf16[192,512]{1,0:T(8,128)(2,1)S(1)}, bf16[192,512]{1,0:T(8,128)(2,1)}, u32[]{:S(2)}) copy-start(bf16[192,512]{1,0:T(8,128)(2,1)} %param.15) | copy-start | bytes 589828
  125.0 8.9 %copy-start.9 = (bf16[192,512]{1,0:T(8,128)(2,1)S(1)}, bf16[192,512]{1,0:T(8,128)(2,1)}, u32[]{:S(2)}) copy-start(bf16[192,512]{1,0:T(8,128)(2,1)} %param.14) | copy-start | bytes 589828
  135.7 1.4 copy-start.10
  288.1 1.2 copy-start.3
  289.2 1.2 copy-start.5
  290.4 1.2 copy-start.1
  291.6 1.1 copy-start.7
  293.4 2.0 copy-start.6
  295.2 1.5 copy-start.8
  295.9 1.8 copy-start.11
  297.7 1.4 copy-start.2
  299.1 1.4 copy-start.4
  301.0 22.7 %copy-start.14 = (bf16[192,512]{1,0:T(8,128)(2,1)S(1)}, bf16[192,512]{1,0:T(8,128)(2,1)}, u32[]{:S(2)}) copy-start(bf16[192,512]{1,0:T(8,128)(2,1)} %param.17) | copy-start | bytes 589828
Sparse Core Ops, SparseCore 0:
  9.4 219.2 all-gather.1
  302.7 20.9 reduce-scatter.1
